TPU v7x, 256 devices: a whole 4x4x8 slice. The times are simulated.
256 devices in a mesh: row: 4 (over y), col: 4 (over x), dp: 16 (over z, core).
Axes of the slice: x: 4, y: 4, z: 8, core: 2. Of those that a mesh axis runs over, the one named last changes fastest.
Arguments:
- hidden_states: bfloat16 [16384, 1536], P(('dp', 'row'), 'col'), may hold values from -18 to 18
- w_query: bfloat16 [1536, 1536], P('col', 'row'), may hold values from -0.102062073 to 0.102062073
- w_key_value: bfloat16 [1536, 512], P('col'), may hold values from -0.102062073 to 0.102062073
- adapter_down: bfloat16 [1024, 1536, 16], P('dp', 'col'), may hold values from -0.15625 to 0.15625
- adapter_up: bfloat16 [1024, 16, 1536], P('dp', None, 'row'), may hold values from -1.5 to 1.5
- req_lengths: int32 [16, 8], replicated, may hold values from 1 to 160, 960 in all within a row
- req_adapter: int32 [16, 8], replicated, may hold values from 0 to 1023, as said below
Outputs:
- attention: bfloat16 [16384, 1536], P(('dp', 'col'), 'row')
- kv_cache: bfloat16 [16384, 512], P(('dp', 'col'))
Inputs may be any that keep to these rules, and one draw needn't show every extreme that they name: `req_lengths`: the lengths of one block sum to 960, and each block has a request of exactly 160 tokens. `req_adapter`: adapters k * 64 to (k + 1) * 64 - 1 are those of index k of dp; the requests of one block use adapters of one index of dp at most 1 times, and some index of dp is used exactly that often by every block.
All inputs are finite; a program needn't handle non-finite values.
Results may differ from a plain program's by a relative error of at most 0.0072.
Values may be sent and summed in bfloat16 or wider, within the bound.
No kernel may reach another device: no remote copies, remote signals or barrier semaphores. Data moves between devices by JAX's collectives and lax.ppermute only.
A program may use at most 128 MiB of HBM per device.

v0:
```python
import math
import jax
import jax.numpy as jnp
from jax import lax
from jax.sharding import PartitionSpec as P

HEAD_DIM = 128
MOST_LEN = 160
masked_score = -1e30


def block_layout(lengths_row, block_len):
    prefix_len = block_len - jnp.sum(lengths_row)
    ends_at = jnp.cumsum(lengths_row) + prefix_len
    starts = ends_at - lengths_row
    positions = jnp.arange(block_len, dtype=jnp.int32)
    segment = jnp.sum((positions[:, None] >= starts[None, :]).astype(jnp.int32), axis=1)
    return (starts, segment, positions)


def slot_numbers(holders):
    request_total = holders.shape[0]
    ordering = jnp.arange(request_total, dtype=jnp.int32)
    earlier = ordering[None, :] < ordering[:, None]
    same_holder = holders[:, None] == holders[None, :]
    return jnp.sum((earlier & same_holder).astype(jnp.int32), axis=1)


def make_attend(query_rows, segment, first_row, kv_group, head_size, kv_half):
    own_rows = query_rows.shape[0]
    heads_here = query_rows.shape[1] // head_size
    query_heads = query_rows.reshape(own_rows, heads_here, head_size)
    query_pos = first_row + jnp.arange(own_rows, dtype=jnp.int32)
    query_seg = lax.dynamic_slice_in_dim(segment, first_row, own_rows, 0)
    score_scale = 1.0 / math.sqrt(head_size)

    def attend(state_in, key_block, key_start):
        running_max, running_sum, running_out = state_in
        block_size = key_block.shape[0]
        key_rows = lax.dynamic_slice_in_dim(key_block, kv_group * head_size, head_size, 1)
        values = lax.dynamic_slice_in_dim(key_block, kv_half + kv_group * head_size, head_size, 1)
        key_pos = jnp.arange(block_size, dtype=jnp.int32)
        allowed = (key_pos[None, :] <= query_pos[:, None]) & (
            (segment[None, :] == query_seg[:, None]) | (segment[None, :] == 0)
        )
        scores = (
            jnp.einsum("qhd,kd->hqk", query_heads, key_rows, preferred_element_type=jnp.float32)
            * score_scale
        )
        scores = jnp.where(allowed[None], scores, masked_score)
        new_max = jnp.maximum(running_max, jnp.max(scores, axis=2))
        weights = jnp.where(allowed[None], jnp.exp(scores - new_max[:, :, None]), 0.0)
        running_sum = jnp.sum(weights, axis=2)
        running_out = jnp.einsum(
            "hqk,kd->hqd", weights.astype(jnp.bfloat16), values, preferred_element_type=jnp.float32
        )
        return (new_max, running_sum, running_out)

    initial = (
        jnp.full((heads_here, own_rows), masked_score, jnp.float32),
        jnp.zeros((heads_here, own_rows), jnp.float32),
        jnp.zeros((heads_here, own_rows, head_size), jnp.float32),
    )
    return (attend, initial)


def body(hidden_states, w_query, w_key_value, adapter_down, adapter_up, req_lengths, req_adapter):
    dp_size = lax.axis_size("dp")
    block_index = lax.axis_index("dp")
    col_index = lax.axis_index("col")
    row_index = lax.axis_index("row")
    gathered = lax.all_gather(hidden_states, "row", axis=0, tiled=True)
    block_len = gathered.shape[0]
    query_cols = w_query.shape[1]
    kv_cols = w_key_value.shape[1]
    kv_half = kv_cols // 2
    head_size = HEAD_DIM
    heads_here = query_cols // head_size
    heads_total = heads_here * lax.axis_size("row")
    kv_heads = kv_half // head_size
    kv_group = row_index * heads_here // (heads_total // kv_heads)
    own_rows = block_len // lax.axis_size("col")
    first_row = col_index * own_rows
    held_sets = adapter_down.shape[0]
    width_here = adapter_down.shape[1]
    rank_size = adapter_down.shape[2]
    lengths_row = req_lengths[block_index]
    adapters_row = req_adapter[block_index]
    requests = lengths_row.shape[0]
    starts, segment, positions = block_layout(lengths_row, block_len)
    request_of = jnp.clip(segment - 1, 0, requests - 1)
    in_request = segment > 0
    holders = adapters_row // held_sets
    slot_of = slot_numbers(holders)
    per_holder = (requests + dp_size - 1) // dp_size
    longest = MOST_LEN
    target_ids = jnp.arange(dp_size, dtype=jnp.int32)[:, None, None]
    slot_ids = jnp.arange(per_holder, dtype=jnp.int32)[None, :, None]
    pairing = (holders[None, None, :] == target_ids) & (slot_of[None, None, :] == slot_ids)
    pair_int = pairing.astype(jnp.int32)
    slot_start = jnp.sum(pair_int * starts[None, None, :], axis=2)
    slot_len = jnp.sum(pair_int * lengths_row[None, None, :], axis=2)
    slot_adapter = jnp.where(
        jnp.any(pairing, axis=2),
        jnp.sum(pair_int * (adapters_row % held_sets)[None, None, :], axis=2),
        -1,
    )
    offsets = jnp.arange(longest, dtype=jnp.int32)
    token_at = slot_start[:, :, None] + offsets[None, None, :]
    live_rows = offsets[None, None, :] < slot_len[:, :, None]
    outgoing = jnp.where(
        live_rows[..., None],
        gathered[jnp.clip(token_at, 0, block_len - 1)],
        jnp.zeros((), gathered.dtype),
    )
    flat_down = jnp.transpose(adapter_down, (1, 0, 2)).reshape(width_here, held_sets * rank_size)
    flat_up = adapter_up.reshape(held_sets * rank_size, query_cols).astype(jnp.float32)
    rank_owner = jnp.arange(held_sets * rank_size, dtype=jnp.int32) // rank_size
    sent_rows = lax.all_to_all(outgoing, "dp", split_axis=0, concat_axis=0, tiled=True)
    sent_ids = lax.all_to_all(
        slot_adapter.astype(jnp.bfloat16), "dp", split_axis=0, concat_axis=0, tiled=True
    )
    reduced = jnp.einsum("nkld,da->nkla", sent_rows, flat_down, preferred_element_type=jnp.float32)
    kept_cols = rank_owner[None, None, :] == sent_ids.astype(jnp.int32)[:, :, None]
    reduced = jnp.where(kept_cols[:, :, None, :], reduced, 0.0)
    adapter_part = jnp.einsum("nkla,af->nklf", reduced, flat_up, precision=lax.Precision.HIGHEST)
    returned = lax.all_to_all(adapter_part, "dp", split_axis=0, concat_axis=0, tiled=True)
    flat_index = (holders[request_of] * per_holder + slot_of[request_of]) * longest + jnp.clip(
        positions - starts[request_of], 0, longest - 1
    )
    adapter_term = returned.reshape(-1, query_cols)[flat_index]
    adapter_term = jnp.where(in_request[:, None], adapter_term, 0.0)
    both_weights = jnp.concatenate([w_query, w_key_value], axis=1)
    partial_value = jnp.dot(gathered, both_weights, preferred_element_type=jnp.float32)
    summed = lax.psum_scatter(
        partial_value
        + jnp.concatenate(
            [adapter_term, jnp.zeros((own_rows * lax.axis_size("col"), kv_cols), jnp.float32)],
            axis=1,
        ),
        "col",
        scatter_dimension=0,
        tiled=True,
    )
    query_rows = summed[:, :query_cols].astype(jnp.bfloat16)
    kv_cache = summed[:, query_cols:].astype(jnp.bfloat16)
    attend, initial = make_attend(query_rows, segment, first_row, kv_group, head_size, kv_half)
    running_max, running_sum, running_out = attend(
        initial, lax.all_gather(kv_cache, "col", axis=0, tiled=True), jnp.int32(0)
    )
    attention = (running_out / running_sum[:, :, None]).astype(jnp.bfloat16)
    attention = jnp.transpose(attention, (1, 0, 2)).reshape(own_rows, query_cols)
    return (attention, kv_cache)


def solution(mesh):
    return jax.shard_map(
        body,
        mesh=mesh,
        in_specs=(
            P(("dp", "row"), "col"),
            P("col", "row"),
            P("col", None),
            P("dp", "col", None),
            P("dp", None, "row"),
            P(),
            P(),
        ),
        out_specs=(P(("dp", "col"), "row"), P(("dp", "col"), None)),
        check_vma=False,
    )
```

profile of v0, /device:TPU:8, one launch (start us, length us, event | category | flops | bytes accessed | tf_op | source)
XLA Modules:
  0.0 303.4 jit_solution(6985747026854632109)
XLA Ops:
  7.2 1.5 fusion.34
  11.0 0.7 copy.46
  11.7 8.6 %all-to-all-start = ((bf16[16,1,1]{2,1,0:T(2,128)(2,1)}), bf16[16,1,1]{2,1,0:T(2,128)(2,1)}, u32[]{:S(2)}, u32[]{:S(2)}) async-start(bf16[16,1,1]{2,1,0:T(2,128)(2,1)} %copy.46), calls=%async_computation | async-start | bytes 16384 | tf_op jit(solution)/shard_map/all_to_all | solution.py:120
  20.5 14.9 %all_gather.6 = bf16[1024,384]{1,0:T(8,128)(2,1)S(1)} all-gather(bf16[256,384]{1,0:T(8,128)(2,1)} %param.7), channel_id=1, replica_groups=mesh['row'=4,'col'=4,'dp'=16] {'row'}, dimensions={0}, use_global_device_ids=true | all-gather | bytes 983040 | tf_op jit(solution)/shard_map/all_gather | solution.py:72
  35.5 7.5 %gather_fusion = bf16[2560,384]{1,0:T(8,128)(2,1)S(1)} fusion(bf16[1024,384]{1,0:T(8,128)(2,1)S(1)} %all_gather.6, s32[3072]{0:T(1024)S(1)} %pad_clamp_fusion), kind=kCustom, calls=%fused_computation | custom fusion | bytes 3942400 | tf_op jit(solution)/shard_map/gather | solution.py:113
  43.0 1.5 broadcast_select_fusion
  44.5 7.0 %all-to-all-start.1 = ((bf16[16,1,160,384]{3,2,1,0:T(8,128)(2,1)}), bf16[16,1,160,384]{3,2,1,0:T(8,128)(2,1)S(1)}, u32[]{:S(2)}, u32[]{:S(2)}) async-start(bf16[16,1,160,384]{3,2,1,0:T(8,128)(2,1)} %broadcast_select_fusion), calls=%async_computation.1 | async-start | bytes 3932160 | tf_op jit(solution)/shard_map/all_to_all | solution.py:119
  51.5 1.1 convert_reduce_fusion.1
  52.7 45.2 %all-to-all-done.1 = bf16[16,1,160,384]{3,2,1,0:T(8,128)(2,1)S(1)} async-done(((bf16[16,1,160,384]{3,2,1,0:T(8,128)(2,1)}), bf16[16,1,160,384]{3,2,1,0:T(8,128)(2,1)S(1)}, u32[]{:S(2)}, u32[]{:S(2)}) %all-to-all-start.1) | async-done | bytes 1966112 | tf_op jit(solution)/shard_map/all_to_all | solution.py:119
  97.9 3.0 fusion.10
  100.9 10.3 %fusion.7 = f32[16,1,160,384]{3,2,1,0:T(8,128)} fusion(bf16[1024,384,1]{1,0,2:T(8,128)(2,1)S(1)} %bitcast.109, f32[16,160,1024]{2,1,0:T(8,128)S(1)} %fusion.10, pred[16,1024]{1,0:T(8,128)(4,1)S(1)} %broadcast_compare_fusion), kind=kOutput, calls=%fused_computation.12 | convolution fusion | flops 12082216960 | bytes 15220736 | tf_op jit(solution)/shard_map/nkla,af->nklf/dot_general | solution.py:126
  111.2 4.8 %all-to-all-start.2 = ((f32[16,1,160,384]{3,2,1,0:T(8,128)}), f32[16,1,160,384]{3,2,1,0:T(8,128)}, u32[]{:S(2)}, u32[]{:S(2)}) async-start(f32[16,1,160,384]{3,2,1,0:T(8,128)} %fusion.7), calls=%async_computation.2 | async-start | bytes 7864320 | tf_op jit(solution)/shard_map/all_to_all | solution.py:127
  116.2 0.7 fusion.52
  117.6 0.7 fusion.53
  118.4 4.1 %select_select_fusion.2 = s32[1024,1]{0,1:T(1,128)S(1)} fusion(s32[]{:T(128)} %bitcast.20, s32[]{:T(128)} %bitcast.21, s32[]{:T(128)} %bitcast.22, s32[]{:T(128)} %bitcast.23, s32[]{:T(128)} %bitcast.24, s32[]{:T(128)} %bitcast.26, s32[]{:T(128)} %bitcast.25, s32[1024,1]{0,1:T(1,128)S(1)} %bitcast.113), kind=kLoop, calls=%fused_computation.56 | loop fusion | flops 15360 | bytes 8220 | tf_op jit(solution)/shard_map/gather | solution.py:128
  122.5 9.0 %select_select_fusion = (s32[1024,1]{0,1:T(1,128)S(1)}, s32[1024,1]{0,1:T(1,128)S(1)}) fusion(s32[]{:T(128)} %bitcast.39, s32[]{:T(128)} %bitcast.40, s32[]{:T(128)} %bitcast.41, s32[]{:T(128)} %bitcast.42, s32[]{:T(128)} %bitcast.43, s32[]{:T(128)} %bitcast.45, s32[]{:T(128)} %bitcast.44, s32[1024,1]{0,1:T(1,128)S(1)} %bitcast.114, s32[]{:T(128)} %bitcast.35, ...), kind=kLoop, calls=%fused_computation.54 | loop fusion | flops 21504 | bytes 12344 | tf_op jit(solution)/shard_map/gather | solution.py:129
  131.6 1.9 broadcast_select_fusion.2
  133.5 71.2 %all-to-all-done.2 = f32[16,1,160,384]{3,2,1,0:T(8,128)} async-done(((f32[16,1,160,384]{3,2,1,0:T(8,128)}), f32[16,1,160,384]{3,2,1,0:T(8,128)}, u32[]{:S(2)}, u32[]{:S(2)}) %all-to-all-start.2) | async-done | bytes 3932192 | tf_op jit(solution)/shard_map/all_to_all | solution.py:127
  204.7 7.1 %gather_fusion.1 = f32[1024,384]{1,0:T(8,128)} fusion(f32[2560,384]{1,0:T(8,128)} %bitcast.17, s32[1024]{0:T(1024)S(1)} %broadcast_clamp_fusion), kind=kCustom, calls=%fused_computation.1 | custom fusion | bytes 3149824 | tf_op jit(solution)/shard_map/gather | solution.py:131
  211.8 1.9 copy.50
  213.9 0.8 copy-done.3
  214.7 3.0 bitcast_add_fusion
  217.8 43.7 %reduce-scatter.2.cloned.1.call-done = f32[256,896]{0,1:T(8,128)} async-done(((f32[1024,896]{0,1:T(8,128)}), f32[256,896]{0,1:T(8,128)}) %reduce-scatter.2.cloned.1.call-update) | async-done | bytes 917520 | tf_op jit(solution)/shard_map/reduce_scatter | solution.py:135
  261.5 1.2 convert.5
  262.7 0.7 slice.41
  263.6 0.8 fusion.18
  264.4 1.8 copy.55
  266.2 25.1 %all-gather.2.cloned.1.call-done = bf16[1024,512]{0,1:T(8,128)(2,1)} async-done(((bf16[256,512]{0,1:T(8,128)(2,1)}), bf16[1024,512]{0,1:T(8,128)(2,1)}) %all-gather.2.cloned.1.call-update) | async-done | bytes 1048592 | tf_op jit(solution)/shard_map/all_gather | solution.py:149
  291.3 1.7 fusion.4
  293.0 0.8 fusion.5
  293.8 1.9 fusion.22
  295.8 0.8 copy.54
  (60 shorter events, 3.4 us)
Async XLA Ops:
  7.2 90.7 %copy-start = (bf16[64,384,16]{1,2,0:T(8,128)(2,1)S(1)}, bf16[64,384,16]{1,2,0:T(8,128)(2,1)}, u32[]{:S(2)}) copy-start(bf16[64,384,16]{1,2,0:T(8,128)(2,1)} %param.10) | copy-start | bytes 2359300
  8.8 11.6 %copy-start.10 = (s32[1,8]{1,0:T(1,128)}, s32[1,8]{1,0:T(1,128)S(1)}, u32[]{:S(2)}) copy-start(s32[1,8]{1,0:T(1,128)S(1)} %copy.62) | copy-start | bytes 100
  8.9 11.4 %copy-start.12 = (s32[8,1]{0,1:T(1,128)}, s32[8,1]{0,1:T(1,128)S(1)}, u32[]{:S(2)}) copy-start(s32[8,1]{0,1:T(1,128)S(1)} %reduce-window.4) | copy-start | bytes 100
  9.0 11.4 %copy-start.6 = (s32[8]{0:T(128)}, s32[8]{0:T(128)S(1)}, u32[]{:S(2)}) copy-start(s32[8]{0:T(128)S(1)} %get-tuple-element.49) | copy-start | bytes 100
  9.1 0.5 copy-start.8
  10.4 0.5 copy-start.4
  11.7 32.8 %all-to-all-start = ((bf16[16,1,1]{2,1,0:T(2,128)(2,1)}), bf16[16,1,1]{2,1,0:T(2,128)(2,1)}, u32[]{:S(2)}, u32[]{:S(2)}) async-start(bf16[16,1,1]{2,1,0:T(2,128)(2,1)} %copy.46), calls=%async_computation | async-start | bytes 16384 | tf_op jit(solution)/shard_map/all_to_all | solution.py:120
  44.5 53.4 %all-to-all-start.1 = ((bf16[16,1,160,384]{3,2,1,0:T(8,128)(2,1)}), bf16[16,1,160,384]{3,2,1,0:T(8,128)(2,1)S(1)}, u32[]{:S(2)}, u32[]{:S(2)}) async-start(bf16[16,1,160,384]{3,2,1,0:T(8,128)(2,1)} %broadcast_select_fusion), calls=%async_computation.1 | async-start | bytes 3932160 | tf_op jit(solution)/shard_map/all_to_all | solution.py:119
  97.9 3.0 copy-start.1
  111.2 5.0 %copy-start.5 = (s32[8]{0:T(128)S(1)}, s32[8]{0:T(128)}, u32[]{:S(2)}) copy-start(s32[8]{0:T(128)} %copy-done.4) | copy-start | bytes 100
  111.2 5.7 %copy-start.9 = (s32[8]{0:T(128)S(1)}, s32[8]{0:T(128)}, u32[]{:S(2)}) copy-start(s32[8]{0:T(128)} %copy-done.8) | copy-start | bytes 100
  111.2 6.4 %copy-start.7 = (s32[8]{0:T(128)S(1)}, s32[8]{0:T(128)}, u32[]{:S(2)}) copy-start(s32[8]{0:T(128)} %copy-done.6) | copy-start | bytes 100
  111.2 7.1 %copy-start.11 = (s32[1,8]{1,0:T(1,128)S(1)}, s32[1,8]{1,0:T(1,128)}, u32[]{:S(2)}) copy-start(s32[1,8]{1,0:T(1,128)} %copy-done.10) | copy-start | bytes 100
  111.2 7.1 %copy-start.13 = (s32[8,1]{0,1:T(1,128)S(1)}, s32[8,1]{0,1:T(1,128)}, u32[]{:S(2)}) copy-start(s32[8,1]{0,1:T(1,128)} %copy-done.12) | copy-start | bytes 100
  111.2 93.5 %all-to-all-start.2 = ((f32[16,1,160,384]{3,2,1,0:T(8,128)}), f32[16,1,160,384]{3,2,1,0:T(8,128)}, u32[]{:S(2)}, u32[]{:S(2)}) async-start(f32[16,1,160,384]{3,2,1,0:T(8,128)} %fusion.7), calls=%async_computation.2 | async-start | bytes 7864320 | tf_op jit(solution)/shard_map/all_to_all | solution.py:127
  116.0 145.5 %reduce-scatter.2.cloned.1.call-start = ((), (), s32[]{:S(2)}) async-start(), calls=%async_computation.4 | async-start | bytes 4587520 | tf_op jit(solution)/shard_map/reduce_scatter | solution.py:135
  211.8 2.1 copy-start.2
  213.8 1.0 copy-start.3
  217.7 73.6 %all-gather.2.cloned.1.call-start = ((), (), s32[]{:S(2)}) async-start(), calls=%async_computation.5 | async-start | bytes 1310720 | tf_op jit(solution)/shard_map/all_gather | solution.py:149
Sparse Core Ops, SparseCore 0:
  217.8 43.6 reduce-scatter.1
  263.6 27.6 all-gather.1
where the time goes:
time: 304 us; the launch traced here: 303 us
  waiting for transfers between devices  185 us (61%)
  local copies, waits for them, and re-layouts  24.7 us (8%)
  other arithmetic  23.1 us (8%)
  starting transfers between devices  20.6 us (7%)
  matrix products  19.9 us (7%)
  between operations  15 us (5%)
  blocking collectives  14.9 us (5%)
    all_to_all x1, waiting for transfers between devices, body(): lax.all_to_all(adapter_part, 'dp', split_axis=0, concat_axis=0, tiled=True)  71.2 us
    all_to_all x1, waiting for transfers between devices, body(): lax.all_to_all(outgoing, 'dp', split_axis=0, concat_axis=0, tiled=True)  45.2 us
    reduce_scatter x1, waiting for transfers between devices, body(): lax.psum_scatter(partial_value + jnp.concatenate([adapter_term, jnp.zeros...  43.7 us
    all_gather x1, waiting for transfers between devices, body(): lax.all_gather(kv_cache, 'col', axis=0, tiled=True)  25.1 us
    all_gather x1, blocking collectives, body(): gathered = lax.all_gather(hidden_states, 'row', axis=0, tiled=True)  14.9 us
    gather x2, other arithmetic, body(): starts[request_of]  10.9 us
    dot_general x1, matrix products, body(): jnp.einsum('nkla,af->nklf', reduced, flat_up, precision=lax.Precision.HIG...  10.3 us
    gather x2, local copies, waits for them, and re-layouts, body(): adapter_term = returned.reshape(-1, query_cols)[flat_index]  9.02 us
  transfers between devices with their start and end apart: 5, of which 4 were waited for; matrix products, arithmetic and copies ran while one was open for 10% of the time, Pallas kernels for 0%

commit v1 on v0

--- a/solution.py
+++ b/solution.py
@@ -7,6 +7,19 @@
 HEAD_DIM = 128
 MOST_LEN = 160
 masked_score = -1e30
+
+
+def ring_gather(value, axis, dim):
+    ways = lax.axis_size(axis)
+    up = [(d, (d + 1) % ways) for d in range(ways)]
+    down = [(d, (d - 1) % ways) for d in range(ways)]
+    earlier, later = ([value], [value])
+    for _ in range(ways // 2):
+        earlier.append(lax.ppermute(earlier[-1], axis, up))
+    for _ in range((ways - 1) // 2):
+        later.append(lax.ppermute(later[-1], axis, down))
+    line = jnp.concatenate([*earlier[::-1], *later[1:]], axis=dim)
+    return jnp.roll(line, (lax.axis_index(axis) - ways // 2) * value.shape[dim], axis=dim)
 
 
 def block_layout(lengths_row, block_len):
@@ -146,7 +159,7 @@
     kv_cache = summed[:, query_cols:].astype(jnp.bfloat16)
     attend, initial = make_attend(query_rows, segment, first_row, kv_group, head_size, kv_half)
     running_max, running_sum, running_out = attend(
-        initial, lax.all_gather(kv_cache, "col", axis=0, tiled=True), jnp.int32(0)
+        initial, ring_gather(kv_cache, "col", 0), jnp.int32(0)
     )
     attention = (running_out / running_sum[:, :, None]).astype(jnp.bfloat16)
     attention = jnp.transpose(attention, (1, 0, 2)).reshape(own_rows, query_cols)

time: 304 us -> 293 us (0.964)
  waiting for transfers between devices: 185 us -> 173 us
  starting transfers between devices: 20.6 us -> 24.2 us
    all_gather x1 -> x0, waiting for transfers between devices: 25.1 us -> none  [body(): lax.all_gather(kv_cache, 'col', axis=0, tiled=True)]
    ppermute x0 -> x3, waiting for transfers between devices: none -> 12.3 us  [the longest x2 12.2 us: ring_gather(): earlier.append(lax.ppermute(earlier[-1], axis, up))]
    ppermute x0 -> x3, starting transfers between devices: none -> 3.62 us  [the longest x1 3.31 us: ring_gather(): later.append(lax.ppermute(later[-1], axis, down))]
  transfers between devices with their start and end apart: 5 -> 7, of which waited for: 4 -> 6; matrix products, arithmetic and copies ran while one was open for 10% -> 10% of each run, Pallas kernels for 0% -> 0%
where the time goes in v1:
time: 293 us; the launch traced here: 291 us
  waiting for transfers between devices  173 us (59%)
  starting transfers between devices  24.2 us (8%)
  local copies, waits for them, and re-layouts  23.3 us (8%)
  other arithmetic  23.1 us (8%)
  matrix products  18.2 us (6%)
  between operations  15 us (5%)
  blocking collectives  14.9 us (5%)
    all_to_all x1, waiting for transfers between devices, body(): lax.all_to_all(adapter_part, 'dp', split_axis=0, concat_axis=0, tiled=True)  71.2 us
    all_to_all x1, waiting for transfers between devices, body(): lax.all_to_all(outgoing, 'dp', split_axis=0, concat_axis=0, tiled=True)  45.2 us
    reduce_scatter x1, waiting for transfers between devices, body(): lax.psum_scatter(partial_value + jnp.concatenate([adapter_term, jnp.zeros...  43.8 us
    all_gather x1, blocking collectives, body(): gathered = lax.all_gather(hidden_states, 'row', axis=0, tiled=True)  14.9 us
    ppermute x2, waiting for transfers between devices, ring_gather(): earlier.append(lax.ppermute(earlier[-1], axis, up))  12.2 us
    gather x2, other arithmetic, body(): starts[request_of]  10.9 us
    dot_general x1, matrix products, body(): jnp.einsum('nkla,af->nklf', reduced, flat_up, precision=lax.Precision.HIG...  10.3 us
    gather x2, local copies, waits for them, and re-layouts, body(): adapter_term = returned.reshape(-1, query_cols)[flat_index]  8.97 us
  transfers between devices with their start and end apart: 7, of which 6 were waited for; matrix products, arithmetic and copies ran while one was open for 10% of the time, Pallas kernels for 0%

profile of v1, /device:TPU:8, one launch (start us, length us, event | category | flops | bytes accessed | tf_op | source)
XLA Modules:
  0.0 291.3 jit_solution(123848767084259276)
XLA Ops:
  7.2 1.5 fusion.34
  11.0 0.7 copy.46
  11.7 8.6 %all-to-all-start = ((bf16[16,1,1]{2,1,0:T(2,128)(2,1)}), bf16[16,1,1]{2,1,0:T(2,128)(2,1)}, u32[]{:S(2)}, u32[]{:S(2)}) async-start(bf16[16,1,1]{2,1,0:T(2,128)(2,1)} %copy.46), calls=%async_computation | async-start | bytes 16384 | tf_op jit(solution)/shard_map/all_to_all | solution.py:133
  20.5 14.9 %all_gather.3 = bf16[1024,384]{1,0:T(8,128)(2,1)S(1)} all-gather(bf16[256,384]{1,0:T(8,128)(2,1)} %param.7), channel_id=1, replica_groups=mesh['row'=4,'col'=4,'dp'=16] {'row'}, dimensions={0}, use_global_device_ids=true | all-gather | bytes 983040 | tf_op jit(solution)/shard_map/all_gather | solution.py:85
  35.5 7.5 %gather_fusion = bf16[2560,384]{1,0:T(8,128)(2,1)S(1)} fusion(bf16[1024,384]{1,0:T(8,128)(2,1)S(1)} %all_gather.3, s32[3072]{0:T(1024)S(1)} %pad_clamp_fusion), kind=kCustom, calls=%fused_computation | custom fusion | bytes 3942400 | tf_op jit(solution)/shard_map/gather | solution.py:126
  43.0 1.5 broadcast_select_fusion
  44.5 7.0 %all-to-all-start.1 = ((bf16[16,1,160,384]{3,2,1,0:T(8,128)(2,1)}), bf16[16,1,160,384]{3,2,1,0:T(8,128)(2,1)S(1)}, u32[]{:S(2)}, u32[]{:S(2)}) async-start(bf16[16,1,160,384]{3,2,1,0:T(8,128)(2,1)} %broadcast_select_fusion), calls=%async_computation.1 | async-start | bytes 3932160 | tf_op jit(solution)/shard_map/all_to_all | solution.py:132
  51.5 1.1 convert_reduce_fusion.1
  52.7 45.2 %all-to-all-done.1 = bf16[16,1,160,384]{3,2,1,0:T(8,128)(2,1)S(1)} async-done(((bf16[16,1,160,384]{3,2,1,0:T(8,128)(2,1)}), bf16[16,1,160,384]{3,2,1,0:T(8,128)(2,1)S(1)}, u32[]{:S(2)}, u32[]{:S(2)}) %all-to-all-start.1) | async-done | bytes 1966112 | tf_op jit(solution)/shard_map/all_to_all | solution.py:132
  97.9 3.0 %fusion.10 = f32[16,160,1024]{2,1,0:T(8,128)S(1)} fusion(bf16[384,1024,1]{0,1,2:T(8,128)(2,1)S(1)} %bitcast.107, bf16[16,1,160,384]{3,2,1,0:T(8,128)(2,1)S(1)} %all-to-all-done.1), kind=kOutput, calls=%fused_computation.13 | convolution fusion | flops 2013265920 | bytes 13238272 | tf_op jit(solution)/shard_map/nkld,da->nkla/dot_general | solution.py:136
  100.9 10.3 %fusion.7 = f32[16,1,160,384]{3,2,1,0:T(8,128)} fusion(bf16[1024,384,1]{1,0,2:T(8,128)(2,1)S(1)} %bitcast.109, f32[16,160,1024]{2,1,0:T(8,128)S(1)} %fusion.10, pred[16,1024]{1,0:T(8,128)(4,1)S(1)} %broadcast_compare_fusion), kind=kOutput, calls=%fused_computation.12 | convolution fusion | flops 12082216960 | bytes 15220736 | tf_op jit(solution)/shard_map/nkla,af->nklf/dot_general | solution.py:139
  111.2 4.8 %all-to-all-start.2 = ((f32[16,1,160,384]{3,2,1,0:T(8,128)}), f32[16,1,160,384]{3,2,1,0:T(8,128)}, u32[]{:S(2)}, u32[]{:S(2)}) async-start(f32[16,1,160,384]{3,2,1,0:T(8,128)} %fusion.7), calls=%async_computation.2 | async-start | bytes 7864320 | tf_op jit(solution)/shard_map/all_to_all | solution.py:140
  116.2 0.7 fusion.50
  118.4 4.1 %select_select_fusion.2 = s32[1024,1]{0,1:T(1,128)S(1)} fusion(s32[]{:T(128)} %bitcast.20, s32[]{:T(128)} %bitcast.21, s32[]{:T(128)} %bitcast.22, s32[]{:T(128)} %bitcast.23, s32[]{:T(128)} %bitcast.24, s32[]{:T(128)} %bitcast.26, s32[]{:T(128)} %bitcast.25, s32[1024,1]{0,1:T(1,128)S(1)} %bitcast.113), kind=kLoop, calls=%fused_computation.64 | loop fusion | flops 15360 | bytes 8220 | tf_op jit(solution)/shard_map/gather | solution.py:141
  122.5 9.0 %select_select_fusion = (s32[1024,1]{0,1:T(1,128)S(1)}, s32[1024,1]{0,1:T(1,128)S(1)}) fusion(s32[]{:T(128)} %bitcast.39, s32[]{:T(128)} %bitcast.40, s32[]{:T(128)} %bitcast.41, s32[]{:T(128)} %bitcast.42, s32[]{:T(128)} %bitcast.43, s32[]{:T(128)} %bitcast.45, s32[]{:T(128)} %bitcast.44, s32[1024,1]{0,1:T(1,128)S(1)} %bitcast.114, s32[]{:T(128)} %bitcast.35, ...), kind=kLoop, calls=%fused_computation.62 | loop fusion | flops 21504 | bytes 12344 | tf_op jit(solution)/shard_map/gather | solution.py:142
  131.6 1.9 broadcast_select_fusion.2
  133.5 71.2 %all-to-all-done.2 = f32[16,1,160,384]{3,2,1,0:T(8,128)} async-done(((f32[16,1,160,384]{3,2,1,0:T(8,128)}), f32[16,1,160,384]{3,2,1,0:T(8,128)}, u32[]{:S(2)}, u32[]{:S(2)}) %all-to-all-start.2) | async-done | bytes 3932192 | tf_op jit(solution)/shard_map/all_to_all | solution.py:140
  204.7 7.1 %gather_fusion.1 = f32[1024,384]{1,0:T(8,128)} fusion(f32[2560,384]{1,0:T(8,128)} %bitcast.17, s32[1024]{0:T(1024)S(1)} %broadcast_clamp_fusion), kind=kCustom, calls=%fused_computation.1 | custom fusion | bytes 3149824 | tf_op jit(solution)/shard_map/gather | solution.py:144
  211.8 1.9 copy.50
  213.9 0.8 copy-done.2
  214.8 3.0 %bitcast_add_fusion = f32[1024,896]{0,1:T(8,128)} fusion(f32[1024,384]{0,1:T(8,128)S(1)} %broadcast_select_fusion.1, bf16[1024,384]{1,0:T(8,128)(2,1)S(1)} %all_gather.3, bf16[384,512]{1,0:T(8,128)(2,1)S(1)} %copy-done.2, bf16[384,384]{1,0:T(8,128)(2,1)S(1)} %copy-done.3), kind=kOutput, calls=%fused_computation.6 | convolution fusion | flops 706936832 | bytes 6717440 | tf_op jit(solution)/shard_map/dot_general | solution.py:147
  217.8 43.8 %reduce-scatter.2.cloned.1.call-done = f32[256,896]{0,1:T(8,128)} async-done(((f32[1024,896]{0,1:T(8,128)}), f32[256,896]{0,1:T(8,128)}) %reduce-scatter.2.cloned.1.call-update) | async-done | bytes 917520 | tf_op jit(solution)/shard_map/reduce_scatter | solution.py:148
  261.6 1.2 convert.5
  263.1 9.0 %collective-permute-done = bf16[256,512]{0,1:T(8,128)(2,1)S(1)} collective-permute-done((bf16[256,512]{0,1:T(8,128)(2,1)S(1)}, bf16[256,512]{0,1:T(8,128)(2,1)S(1)}, u32[]{:S(2)}, u32[]{:S(2)}) %collective-permute-start) | collective-permute-done | bytes 262176 | tf_op jit(solution)/shard_map/ppermute | solution.py:18
  272.2 0.8 fusion.18
  273.0 3.3 %collective-permute-start.2 = (bf16[256,512]{0,1:T(8,128)(2,1)S(1)}, bf16[256,512]{0,1:T(8,128)(2,1)S(1)}, u32[]{:S(2)}, u32[]{:S(2)}) collective-permute-start(bf16[256,512]{0,1:T(8,128)(2,1)S(1)} %slice.41), channel_id=1, source_target_pairs={{0,48},{16,0},{32,16},{48,32},{1,49},{17,1},{33,17},{49,33},{2,50}... | collective-permute-start | bytes 786440 | tf_op jit(solution)/shard_map/ppermute | solution.py:20
  276.3 0.8 copy.55
  277.1 3.3 %collective-permute-done.1 = bf16[256,512]{0,1:T(8,128)(2,1)S(1)} collective-permute-done((bf16[256,512]{0,1:T(8,128)(2,1)S(1)}, bf16[256,512]{0,1:T(8,128)(2,1)S(1)}, u32[]{:S(2)}, u32[]{:S(2)}) %collective-permute-start.1) | collective-permute-done | bytes 262176 | tf_op jit(solution)/shard_map/ppermute | solution.py:18
  280.8 0.9 fusion.4
  281.7 0.8 fusion.5
  282.5 1.1 fusion.22
  283.6 0.8 copy.54
  (71 shorter events, 4.8 us)
Async XLA Ops:
  7.2 90.7 %copy-start = (bf16[64,384,16]{1,2,0:T(8,128)(2,1)S(1)}, bf16[64,384,16]{1,2,0:T(8,128)(2,1)}, u32[]{:S(2)}) copy-start(bf16[64,384,16]{1,2,0:T(8,128)(2,1)} %param.10) | copy-start | bytes 2359300
  8.8 11.6 %copy-start.10 = (s32[1,8]{1,0:T(1,128)}, s32[1,8]{1,0:T(1,128)S(1)}, u32[]{:S(2)}) copy-start(s32[1,8]{1,0:T(1,128)S(1)} %copy.62) | copy-start | bytes 100
  8.9 11.4 %copy-start.12 = (s32[8,1]{0,1:T(1,128)}, s32[8,1]{0,1:T(1,128)S(1)}, u32[]{:S(2)}) copy-start(s32[8,1]{0,1:T(1,128)S(1)} %reduce-window.4) | copy-start | bytes 100
  9.0 11.4 %copy-start.6 = (s32[8]{0:T(128)}, s32[8]{0:T(128)S(1)}, u32[]{:S(2)}) copy-start(s32[8]{0:T(128)S(1)} %get-tuple-element.49) | copy-start | bytes 100
  9.1 0.5 copy-start.8
  10.4 0.5 copy-start.4
  11.7 32.8 %all-to-all-start = ((bf16[16,1,1]{2,1,0:T(2,128)(2,1)}), bf16[16,1,1]{2,1,0:T(2,128)(2,1)}, u32[]{:S(2)}, u32[]{:S(2)}) async-start(bf16[16,1,1]{2,1,0:T(2,128)(2,1)} %copy.46), calls=%async_computation | async-start | bytes 16384 | tf_op jit(solution)/shard_map/all_to_all | solution.py:133
  44.5 53.4 %all-to-all-start.1 = ((bf16[16,1,160,384]{3,2,1,0:T(8,128)(2,1)}), bf16[16,1,160,384]{3,2,1,0:T(8,128)(2,1)S(1)}, u32[]{:S(2)}, u32[]{:S(2)}) async-start(bf16[16,1,160,384]{3,2,1,0:T(8,128)(2,1)} %broadcast_select_fusion), calls=%async_computation.1 | async-start | bytes 3932160 | tf_op jit(solution)/shard_map/all_to_all | solution.py:132
  97.9 3.0 %copy-start.1 = (bf16[64,16,384]{2,1,0:T(8,128)(2,1)S(1)}, bf16[64,16,384]{2,1,0:T(8,128)(2,1)}, u32[]{:S(2)}) copy-start(bf16[64,16,384]{2,1,0:T(8,128)(2,1)} %param.11) | copy-start | bytes 2359300
  111.2 5.0 %copy-start.5 = (s32[8]{0:T(128)S(1)}, s32[8]{0:T(128)}, u32[]{:S(2)}) copy-start(s32[8]{0:T(128)} %copy-done.4) | copy-start | bytes 100
  111.2 5.7 %copy-start.9 = (s32[8]{0:T(128)S(1)}, s32[8]{0:T(128)}, u32[]{:S(2)}) copy-start(s32[8]{0:T(128)} %copy-done.8) | copy-start | bytes 100
  111.2 6.4 %copy-start.7 = (s32[8]{0:T(128)S(1)}, s32[8]{0:T(128)}, u32[]{:S(2)}) copy-start(s32[8]{0:T(128)} %copy-done.6) | copy-start | bytes 100
  111.2 7.1 %copy-start.11 = (s32[1,8]{1,0:T(1,128)S(1)}, s32[1,8]{1,0:T(1,128)}, u32[]{:S(2)}) copy-start(s32[1,8]{1,0:T(1,128)} %copy-done.10) | copy-start | bytes 100
  111.2 7.1 %copy-start.13 = (s32[8,1]{0,1:T(1,128)S(1)}, s32[8,1]{0,1:T(1,128)}, u32[]{:S(2)}) copy-start(s32[8,1]{0,1:T(1,128)} %copy-done.12) | copy-start | bytes 100
  111.2 93.5 %all-to-all-start.2 = ((f32[16,1,160,384]{3,2,1,0:T(8,128)}), f32[16,1,160,384]{3,2,1,0:T(8,128)}, u32[]{:S(2)}, u32[]{:S(2)}) async-start(f32[16,1,160,384]{3,2,1,0:T(8,128)} %fusion.7), calls=%async_computation.2 | async-start | bytes 7864320 | tf_op jit(solution)/shard_map/all_to_all | solution.py:140
  116.0 145.6 %reduce-scatter.2.cloned.1.call-start = ((), (), s32[]{:S(2)}) async-start(), calls=%async_computation.4 | async-start | bytes 4587520 | tf_op jit(solution)/shard_map/reduce_scatter | solution.py:148
  213.7 1.0 copy-start.2
  213.7 1.1 copy-start.3
  262.8 9.3 %collective-permute-start = (bf16[256,512]{0,1:T(8,128)(2,1)S(1)}, bf16[256,512]{0,1:T(8,128)(2,1)S(1)}, u32[]{:S(2)}, u32[]{:S(2)}) collective-permute-start(bf16[256,512]{0,1:T(8,128)(2,1)S(1)} %slice.41), channel_id=1, source_target_pairs={{0,16},{16,32},{32,48},{48,0},{1,17},{17,33},{33,49},{49,1},{2,18}... | collective-permute-start | bytes 786440 | tf_op jit(solution)/shard_map/ppermute | solution.py:18
  272.1 8.3 %collective-permute-start.1 = (bf16[256,512]{0,1:T(8,128)(2,1)S(1)}, bf16[256,512]{0,1:T(8,128)(2,1)S(1)}, u32[]{:S(2)}, u32[]{:S(2)}) collective-permute-start(bf16[256,512]{0,1:T(8,128)(2,1)S(1)} %collective-permute-done), channel_id=1, source_target_pairs={{0,16},{16,32},{32,48},{48,0},{1,17},{17,33},{33,49},{49,1},{2,18}... | collective-permute-start | bytes 786440 | tf_op jit(solution)/shard_map/ppermute | solution.py:18
  273.0 7.7 %collective-permute-start.2 = (bf16[256,512]{0,1:T(8,128)(2,1)S(1)}, bf16[256,512]{0,1:T(8,128)(2,1)S(1)}, u32[]{:S(2)}, u32[]{:S(2)}) collective-permute-start(bf16[256,512]{0,1:T(8,128)(2,1)S(1)} %slice.41), channel_id=1, source_target_pairs={{0,48},{16,0},{32,16},{48,32},{1,49},{17,1},{33,17},{49,33},{2,50}... | collective-permute-start | bytes 786440 | tf_op jit(solution)/shard_map/ppermute | solution.py:20
Sparse Core Ops, SparseCore 0:
  217.9 43.6 reduce-scatter.1
